TPU v7x, 256 devices: a whole 4x4x8 slice. The times are simulated.
256 devices in a mesh: tile: 16 (over z, x_lo), obj: 16 (over x_hi, y, core).
Axes of the slice: x: 4 (x_hi: 2, x_lo: 2; x = x_hi * 2 + x_lo), y: 4, z: 8, core: 2. Of those that a mesh axis runs over, the one named last changes fastest.
Arguments:
- adjoint_in: float32 [256, 2, 256, 1024], P('obj', None, 'tile'), may hold values from -6 to 6
- checkpoint_store: float32 [64, 2, 256, 1024], P('obj', None, 'tile'), may hold values from 1900 to 2500, as said below
- interval: int32 [1], replicated, may hold values from 0 to 63
- sea_mask: int32 [256, 1024], P('tile'), may hold values 0 or 1
- zonal_speed: float32 [256, 1024], P('tile'), may hold values from -0.45 to 0.45
- mixing: float32 [256, 1024], P('tile'), may hold values from 0.02 to 0.2
- piston: float32 [256, 32], P('tile'), may hold values from 0.1 to 0.9
- cell_area: float32 [256, 32], P('tile'), may hold values from 5 to 50
- region: int32 [256, 32], P('tile'), may hold values from 0 to 255
Outputs:
- adjoint_out: float32 [256, 2, 256, 1024], P('obj', None, 'tile')
Inputs may be any that keep to these rules, and one draw needn't show every extreme that they name: region numbers name objectives. `checkpoint_store`: dissolved carbon lies in 1900 to 2100 and alkalinity exceeds it by 200 to 400 in every cell.
All inputs are finite; a program needn't handle non-finite values. No bound on the sum of `sea_mask` on one device may be relied on, other than what follows from the above.
Results may differ from a plain program's by a relative error of at most 0.0003.
Values sent between devices are 32-bit elements; how exact they have to be, the bound alone decides.
No kernel may reach another device: no remote copies, remote signals or barrier semaphores. Data moves between devices by JAX's collectives and lax.ppermute only.
A program may use at most 64 MiB of HBM per device.

v0:
```python
import jax
import jax.numpy as jnp
from jax import lax
from jax.sharding import PartitionSpec as P

ROWS = 32
LEVELS = 32
NEWTON = 4
DISSOCIATION_ONE = 1400.0
DISSOCIATION_TWO = 1.1
BORATE_CONSTANT = 2.5
BORON_TOTAL = 416.0
AIR_CARBON = 14.0
START_HYDROGEN = 2.0
ROW_DIFFUSION = 0.1


def padded(cells, sides, width):
    for axis, dim in sides:
        count = lax.axis_size(axis)
        head = lax.slice_in_dim(cells, 0, width, axis=dim)
        tail = lax.slice_in_dim(cells, cells.shape[dim] - width, cells.shape[dim], axis=dim)
        cells = jnp.concatenate(
            [
                lax.ppermute(tail, axis, [(i, (i + 1) % count) for i in range(count)]),
                cells,
                lax.ppermute(head, axis, [((i + 1) % count, i) for i in range(count)]),
            ],
            axis=dim,
        )
    return cells


def spread(value, axis, source):
    kept = jnp.where(lax.axis_index(axis) == source, value, 0).astype(value.dtype)
    return lax.psum(kept, axis)


def chemistry(carbon, alkalinity, piston, surface_sea):
    hydrogen = jnp.full_like(carbon, START_HYDROGEN)
    for iteration in range(NEWTON):
        square = hydrogen * hydrogen
        denominator = square + DISSOCIATION_ONE * hydrogen + DISSOCIATION_ONE * DISSOCIATION_TWO
        carbonate = carbon * DISSOCIATION_ONE * (hydrogen + 2.0 * DISSOCIATION_TWO) / denominator
        borate = BORON_TOTAL * BORATE_CONSTANT / (hydrogen + BORATE_CONSTANT)
        derivative = -carbon * DISSOCIATION_ONE * (
            square + 4.0 * DISSOCIATION_TWO * hydrogen + DISSOCIATION_ONE * DISSOCIATION_TWO
        ) / (denominator * denominator) - borate / (hydrogen + BORATE_CONSTANT)
        hydrogen = hydrogen - (carbonate + borate - alkalinity) / derivative
    square = hydrogen * hydrogen
    denominator = square + DISSOCIATION_ONE * hydrogen + DISSOCIATION_ONE * DISSOCIATION_TWO
    dissolved = carbon * square / denominator
    return surface_sea * piston * (AIR_CARBON - dissolved)


def forward_shift(source, offset):
    padding = jnp.zeros(source.shape[:-1] + (offset,), source.dtype)
    return jnp.concatenate([source[..., offset:], padding], axis=-1)


def backward_shift(source, offset):
    padding = jnp.zeros(source.shape[:-1] + (offset,), source.dtype)
    return jnp.concatenate([padding, source[..., :-offset]], axis=-1)


def column_weights(sea_float, mixing):
    cell_index = jnp.arange(LEVELS * ROWS, dtype=jnp.int32)
    row_open = (cell_index % ROWS < ROWS - 1).astype(jnp.float32)
    level_open = (cell_index // ROWS < LEVELS - 1).astype(jnp.float32)
    row_weight = ROW_DIFFUSION * row_open * sea_float * forward_shift(sea_float, 1)
    level_weight = mixing * level_open * sea_float * forward_shift(sea_float, ROWS)
    return (row_weight, level_weight)


def column_mix(source, row_weight, level_weight):
    row_flux = row_weight * (forward_shift(source, 1) - source)
    level_flux = level_weight * (forward_shift(source, ROWS) - source)
    return row_flux - backward_shift(row_flux, 1) + level_flux - backward_shift(level_flux, ROWS)


def zonal_weights(sea_float, sea_east, velocity):
    opened = sea_float * sea_east
    magnitude = jnp.abs(velocity)
    return jnp.stack(
        [
            opened * (-velocity - magnitude) / 12.0,
            opened * (7.0 * velocity + 3.0 * magnitude) / 12.0,
            opened * (7.0 * velocity - 3.0 * magnitude) / 12.0,
            opened * (magnitude - velocity) / 12.0,
        ]
    )


def trim_rim(source, keep_rim, outer_rim, dimension):
    length = source.shape[dimension] - 2 * outer_rim
    return lax.slice_in_dim(
        source, outer_rim - keep_rim, outer_rim + length + keep_rim, axis=dimension
    )


def surface_slopes(carbon, alkalinity, piston, surface_sea):

    def uptake_of(carbon_in, alkalinity_in):
        return chemistry(carbon_in, alkalinity_in, piston, surface_sea)

    uptake, pullback = jax.vjp(uptake_of, carbon, alkalinity)
    by_carbon, by_alkalinity = pullback(jnp.ones_like(carbon))
    return (uptake, jnp.stack([by_carbon, by_alkalinity]))


def advance_rim(extended, weights, row_weight, level_weight, uptake):
    length = extended.shape[1]
    face_flux = (
        weights[0, 1 : length - 2] * extended[:, 0 : length - 3]
        + weights[1, 1 : length - 2] * extended[:, 1 : length - 2]
        + weights[2, 1 : length - 2] * extended[:, 2 : length - 1]
        + weights[3, 1 : length - 2] * extended[:, 3:length]
    )
    interior = extended[:, 2 : length - 2]
    zonal_term = -(face_flux[:, 1:] - face_flux[:, :-1])
    transported = interior + zonal_term + column_mix(interior, row_weight, level_weight)
    surface_row = transported[0, :, :ROWS] + uptake
    carbon = jnp.concatenate([surface_row, transported[0, :, ROWS:]], axis=-1)
    return jnp.stack([carbon, transported[1]])


def retreat(extended, weights, row_weight, level_weight, slopes, objective_seeds):
    length = extended.shape[2]
    difference = extended[:, :, 1:] - extended[:, :, :-1]
    zonal_term = (
        weights[0, 3 : length - 1] * difference[:, :, 3 : length - 1]
        + weights[1, 2 : length - 2] * difference[:, :, 2 : length - 2]
        + weights[2, 1 : length - 3] * difference[:, :, 1 : length - 3]
        + weights[3, 0 : length - 4] * difference[:, :, 0 : length - 4]
    )
    interior = extended[:, :, 2 : length - 2]
    adjoint = interior + zonal_term + column_mix(interior, row_weight, level_weight)
    forcing = interior[:, 0, :, :ROWS] + objective_seeds
    surface = adjoint[..., :ROWS] + slopes[None] * forcing[:, None]
    return jnp.concatenate([surface, adjoint[..., ROWS:]], axis=-1)


def body(
    adjoint_in, checkpoint_store, interval, sea_mask, zonal_speed, mixing, piston, cell_area, region
):
    groups = adjoint_in.shape[0]
    cell_count = adjoint_in.shape[3]
    rim_depth = 2
    statics = jnp.concatenate(
        [
            sea_mask.astype(jnp.float32),
            zonal_speed,
            mixing,
            piston,
            cell_area,
            region.astype(jnp.float32),
        ],
        axis=1,
    )
    widened = padded(statics, (("tile", 0),), rim_depth)
    sea_wide = widened[:, :cell_count]
    speed_wide = widened[:, cell_count : 2 * cell_count]
    mixing_wide = widened[:, 2 * cell_count : 3 * cell_count]
    offset = 3 * cell_count
    piston_wide = widened[:, offset : offset + ROWS]
    area_wide = widened[:, offset + ROWS : offset + 2 * ROWS]
    region_wide = widened[:, offset + 2 * ROWS : offset + 3 * ROWS]
    sea_east = jnp.concatenate([sea_wide[1:], jnp.zeros_like(sea_wide[:1])], axis=0)
    weights = zonal_weights(sea_wide, sea_east, speed_wide)
    row_weight, level_weight = column_weights(sea_wide, mixing_wide)
    surface_sea = sea_wide[:, :ROWS]
    targets = (lax.axis_index("obj") * groups + jnp.arange(groups, dtype=jnp.int32)).astype(
        jnp.float32
    )
    objective_seeds = area_wide[None] * (region_wide[None] == targets[:, None, None]).astype(
        jnp.float32
    )
    owners = lax.axis_size("obj")
    owner_index = interval[0] % owners
    stored = lax.dynamic_index_in_dim(checkpoint_store, interval[0] // owners, 0, keepdims=False)
    linearize_extended = padded(spread(stored, "obj", owner_index), (("tile", 1),), rim_depth)
    inner_rim = rim_depth - 2
    piston_inner = trim_rim(piston_wide, inner_rim, rim_depth, 0)
    sea_inner = trim_rim(surface_sea, inner_rim, rim_depth, 0)
    initial_inner = trim_rim(linearize_extended, inner_rim, rim_depth, 1)
    uptake_first, slopes_first = surface_slopes(
        initial_inner[0, :, :ROWS], initial_inner[1, :, :ROWS], piston_inner, sea_inner
    )
    following = advance_rim(
        linearize_extended,
        weights,
        trim_rim(row_weight, inner_rim, rim_depth, 0),
        trim_rim(level_weight, inner_rim, rim_depth, 0),
        uptake_first,
    )
    _, slopes_second = surface_slopes(
        following[0, :, :ROWS], following[1, :, :ROWS], piston_inner, sea_inner
    )
    slopes = jnp.stack([slopes_first, slopes_second])
    adjoint = adjoint_in
    for substep in (1, 0):
        extended = padded(adjoint, (("tile", 2),), 2)
        rim_in = 0 + 2
        adjoint = retreat(
            extended,
            trim_rim(weights, rim_in, rim_depth, 1),
            trim_rim(row_weight, 0, rim_depth, 0),
            trim_rim(level_weight, 0, rim_depth, 0),
            trim_rim(slopes[substep], 0, rim_depth - 2, 1),
            trim_rim(objective_seeds, 0, rim_depth, 1),
        )
    return adjoint


def solution(mesh):
    placed = (
        P("obj", None, "tile", None),
        P("obj", None, "tile", None),
        P(),
        P("tile", None),
        P("tile", None),
        P("tile", None),
        P("tile", None),
        P("tile", None),
        P("tile", None),
    )
    return jax.shard_map(
        body, mesh=mesh, in_specs=placed, out_specs=P("obj", None, "tile", None), check_vma=False
    )
```

profile of v0, /device:TPU:1, one launch (start us, length us, event | category | flops | bytes accessed | tf_op | source)
XLA Modules:
  0.0 209.7 jit_solution(15050452365637785768)
XLA Ops:
  6.5 0.0 all-reduce.17.cloned.1.call-start
  7.2 1.6 select_bitcast_fusion
  8.8 0.0 all-reduce.17.cloned.1.call-update
  8.8 0.7 convert_element_type.25
  9.5 0.8 convert_element_type.24
  10.4 1.0 concatenate.75
  11.3 2.1 %collective-permute-start = (f32[2,3168]{1,0:T(2,128)S(1)}, f32[2,3168]{1,0:T(2,128)S(1)}, u32[]{:S(2)}, u32[]{:S(2)}) collective-permute-start(f32[2,3168]{1,0:T(2,128)S(1)} %get-tuple-element.39), channel_id=1, source_target_pairs={{0,16},{16,32},{32,48},{48,64},{64,80},{80,96},{96,112},{112,128},... | collective-permute-start | bytes 76040 | tf_op jit(solution)/shard_map/ppermute | solution.py:25
  13.4 5.4 %collective-permute-start.1 = (f32[2,3168]{1,0:T(2,128)S(1)}, f32[2,3168]{1,0:T(2,128)S(1)}, u32[]{:S(2)}, u32[]{:S(2)}) collective-permute-start(f32[2,3168]{1,0:T(2,128)S(1)} %get-tuple-element.40), channel_id=1, source_target_pairs={{16,0},{32,16},{48,32},{64,48},{80,64},{96,80},{112,96},{128,112},... | collective-permute-start | bytes 76040 | tf_op jit(solution)/shard_map/ppermute | solution.py:27
  18.8 2.8 %copy.14 = f32[16,2,16,1024]{3,0,2,1:T(8,128)S(1)} copy(f32[16,2,16,1024]{3,2,1,0:T(8,128)} %param.9) | data formatting | bytes 4194304 | tf_op args[0]
  21.6 0.9 fusion.63
  22.5 1.4 collective-permute-start.3
  23.9 0.1 collective-permute-start.2
  24.0 2.0 slice.328
  25.9 1.9 slice.322
  27.9 0.0 collective-permute-done
  27.9 0.0 collective-permute-done.1
  27.9 0.1 slice.320
  28.0 0.1 slice.325
  28.1 0.1 multiply_bitcast_fusion.1
  28.2 0.0 copy-start.3
  28.3 0.1 pad_maximum_fusion.8
  28.4 0.1 select_add_fusion
  28.6 133.8 %all-reduce.17.cloned.1.call-done = f32[2,16,1024]{2,1,0:T(8,128)} async-done(((f32[2,16,1024]{2,1,0:T(8,128)}), f32[2,16,1024]{2,1,0:T(8,128)}) %all-reduce.17.cloned.1.call-update) | async-done | bytes 131088 | tf_op jit(solution)/shard_map/psum | solution.py:36
  162.3 0.9 fusion.65
  163.3 0.4 collective-permute-start.4
  163.6 3.3 %collective-permute-start.5 = (f32[2,2,1024]{2,1,0:T(2,128)S(1)}, f32[2,2,1024]{2,1,0:T(2,128)S(1)}, u32[]{:S(2)}, u32[]{:S(2)}) collective-permute-start(f32[2,2,1024]{2,1,0:T(2,128)S(1)} %get-tuple-element.47), channel_id=1, source_target_pairs={{16,0},{32,16},{48,32},{64,48},{80,64},{96,80},{112,96},{128,112},... | collective-permute-start | bytes 49160 | tf_op jit(solution)/shard_map/ppermute | solution.py:27
  166.9 1.0 slice.346
  167.9 1.0 slice.344
  168.9 0.0 copy-start
  168.9 0.0 copy-start.1
  168.9 1.1 subtract_multiply_fusion.5
  170.0 0.0 copy-done.3
  170.1 1.1 add_bitcast_fusion.1
  171.1 0.0 collective-permute-done.5
  171.1 0.0 collective-permute-done.4
  171.2 1.1 fusion.13
  172.2 0.0 copy-done.2
  172.3 0.1 fusion.19
  172.4 0.1 slice_bitcast_fusion.6
  172.5 0.1 add_bitcast_fusion
  172.5 0.1 maximum_bitcast_fusion
  172.6 0.1 add_bitcast_fusion.3
  172.8 0.0 collective-permute-done.2
  172.9 0.0 copy-done
  172.9 0.0 copy-done.1
  172.9 3.5 %subtract_multiply_fusion.3 = (f32[16,2,16,1024]{3,0,2,1:T(8,128)S(1)}, f32[16,2,20,1024]{3,0,2,1:T(8,128)S(1)}, f32[16,2,16,1024]{3,0,2,1:T(8,128)S(1)}) fusion(f32[16,2,16,1023]{3,0,2,1:T(8,128)} %slice.322, f32[16,1024]{1,0:T(8,128)S(1)} %get-tuple-element.48, f32[16,2,16,1024]{3,2,1,0:T(8,128)S(1)} %copy-done, ...), kind=kLoop, calls=%fused_computation.30 | loop fusion | flops 2097152 | bytes 12711936 | tf_op jit(solution)/shard_map/mul | solution.py:76
  176.4 0.0 collective-permute-done.3
  176.4 0.3 slice_subtract_fusion.1
  176.8 4.4 %fusion.8 = f32[16,2,16,1024]{3,0,2,1:T(8,128)S(1)} fusion(f32[16,2,19,1024]{3,0,2,1:T(8,128)S(1)} %slice_subtract_fusion.1, f32[16,2,16,992]{3,0,2,1:T(8,128)S(1)} %bitcast.349, f32[16,2,16,1024]{3,0,2,1:T(8,128)S(1)} %get-tuple-element.29, f32[16,2,16,1024]{3,0,2,1:T(8,128)S(1)} %get-tuple-element.27, f32[16,2,16,1023]{3,0,2,1:T(8,128)S(1)} %bitcast.348, ...), kind=kLoop, calls=%fused_computation.20 | loop fusion | flops 6291456 | bytes 21166080 | tf_op jit(solution)/shard_map/add | solution.py:137
  181.2 0.6 slice.357
  181.9 0.2 fusion.11
  182.1 0.7 fusion
  182.8 0.1 collective-permute-start.6
  182.8 3.6 %collective-permute-start.7 = (f32[16,2,2,1024]{3,0,2,1:T(8,128)S(1)}, f32[16,2,2,1024]{3,0,2,1:T(8,128)S(1)}, u32[]{:S(2)}, u32[]{:S(2)}) collective-permute-start(f32[16,2,2,1024]{3,0,2,1:T(8,128)S(1)} %get-tuple-element.26), channel_id=1, source_target_pairs={{16,0},{32,16},{48,32},{64,48},{80,64},{96,80},{112,96},{128,112},... | collective-permute-start | bytes 786440 | tf_op jit(solution)/shard_map/ppermute | solution.py:27
  186.4 1.2 subtract_multiply_fusion.1
  187.7 0.1 select_add_fusion.1
  187.7 5.3 %collective-permute-done.6 = f32[16,2,2,1024]{3,0,2,1:T(8,128)S(1)} collective-permute-done((f32[16,2,2,1024]{3,0,2,1:T(8,128)S(1)}, f32[16,2,2,1024]{3,0,2,1:T(8,128)S(1)}, u32[]{:S(2)}, u32[]{:S(2)}) %collective-permute-start.6) | collective-permute-done | bytes 262176 | tf_op jit(solution)/shard_map/ppermute | solution.py:25
  193.1 2.2 %collective-permute-done.7 = f32[16,2,2,1024]{3,0,2,1:T(8,128)S(1)} collective-permute-done((f32[16,2,2,1024]{3,0,2,1:T(8,128)S(1)}, f32[16,2,2,1024]{3,0,2,1:T(8,128)S(1)}, u32[]{:S(2)}, u32[]{:S(2)}) %collective-permute-start.7) | collective-permute-done | bytes 262176 | tf_op jit(solution)/shard_map/ppermute | solution.py:27
  195.3 0.6 pad_maximum_fusion.1
  195.9 0.2 slice_subtract_fusion
  196.1 2.9 %fusion.3 = f32[16,2,16,1024]{3,0,2,1:T(8,128)S(1)} fusion(f32[16,2,19,1024]{3,0,2,1:T(8,128)S(1)} %slice_subtract_fusion, f32[16,2,16,992]{3,0,2,1:T(8,128)S(1)} %bitcast.350, f32[16,2,16,1024]{3,0,2,1:T(8,128)S(1)} %get-tuple-element.23, f32[16,2,16,1023]{3,0,2,1:T(8,128)S(1)} %bitcast.347, f32[16,2,16,992]{3,0,2,1:T(8,128)S(1)} %slice.357, ...), kind=kLoop, calls=%fused_computation.11 | loop fusion | flops 7864320 | bytes 19134464 | tf_op jit(solution)/shard_map/add | solution.py:137
  199.1 0.6 slice.374
  199.8 0.6 pad_maximum_fusion.2
  200.4 2.5 %copy.20 = f32[16,2,16,1024]{3,2,1,0:T(8,128)} copy(f32[16,2,16,1024]{3,0,2,1:T(8,128)S(1)} %pad_maximum_fusion.2) | data formatting | bytes 4194304 | tf_op jit(solution)/shard_map/concatenate | solution.py:140
  (23 shorter events, 0.4 us)
Async XLA Ops:
  6.5 155.8 %all-reduce.17.cloned.1.call-start = ((), (), s32[]{:S(2)}) async-start(), calls=%async_computation | async-start | bytes 262144 | tf_op jit(solution)/shard_map/psum | solution.py:36
  11.3 16.5 %collective-permute-start = (f32[2,3168]{1,0:T(2,128)S(1)}, f32[2,3168]{1,0:T(2,128)S(1)}, u32[]{:S(2)}, u32[]{:S(2)}) collective-permute-start(f32[2,3168]{1,0:T(2,128)S(1)} %get-tuple-element.39), channel_id=1, source_target_pairs={{0,16},{16,32},{32,48},{48,64},{64,80},{80,96},{96,112},{112,128},... | collective-permute-start | bytes 76040 | tf_op jit(solution)/shard_map/ppermute | solution.py:25
  13.4 14.4 %collective-permute-start.1 = (f32[2,3168]{1,0:T(2,128)S(1)}, f32[2,3168]{1,0:T(2,128)S(1)}, u32[]{:S(2)}, u32[]{:S(2)}) collective-permute-start(f32[2,3168]{1,0:T(2,128)S(1)} %get-tuple-element.40), channel_id=1, source_target_pairs={{16,0},{32,16},{48,32},{64,48},{80,64},{96,80},{112,96},{128,112},... | collective-permute-start | bytes 76040 | tf_op jit(solution)/shard_map/ppermute | solution.py:27
  22.5 153.9 %collective-permute-start.3 = (f32[16,2,2,1024]{3,0,2,1:T(8,128)}, f32[16,2,2,1024]{3,0,2,1:T(8,128)S(1)}, u32[]{:S(2)}, u32[]{:S(2)}) collective-permute-start(f32[16,2,2,1024]{3,0,2,1:T(8,128)} %get-tuple-element.30), channel_id=1, source_target_pairs={{16,0},{32,16},{48,32},{64,48},{80,64},{96,80},{112,96},{128,112},... | collective-permute-start | bytes 786440 | tf_op jit(solution)/shard_map/ppermute | solution.py:27
  23.9 149.0 %collective-permute-start.2 = (f32[16,2,2,1024]{3,0,2,1:T(8,128)}, f32[16,2,2,1024]{3,0,2,1:T(8,128)S(1)}, u32[]{:S(2)}, u32[]{:S(2)}) collective-permute-start(f32[16,2,2,1024]{3,0,2,1:T(8,128)} %get-tuple-element.31), channel_id=1, source_target_pairs={{0,16},{16,32},{32,48},{48,64},{64,80},{80,96},{96,112},{112,128},... | collective-permute-start | bytes 786440 | tf_op jit(solution)/shard_map/ppermute | solution.py:25
  28.2 141.8 %copy-start.3 = (f32[16,32]{1,0:T(8,128)S(1)}, f32[16,32]{1,0:T(8,128)}, u32[]{:S(2)}) copy-start(f32[16,32]{1,0:T(8,128)} %param.15) | copy-start | bytes 6148
  162.3 9.9 %copy-start.2 = (f32[2,16,1024]{2,1,0:T(8,128)S(1)}, f32[2,16,1024]{2,1,0:T(8,128)}, u32[]{:S(2)}) copy-start(f32[2,16,1024]{2,1,0:T(8,128)} %all-reduce.17.cloned.1.call-done) | copy-start | bytes 393220
  163.3 7.9 %collective-permute-start.4 = (f32[2,2,1024]{2,1,0:T(2,128)S(1)}, f32[2,2,1024]{2,1,0:T(2,128)S(1)}, u32[]{:S(2)}, u32[]{:S(2)}) collective-permute-start(f32[2,2,1024]{2,1,0:T(2,128)S(1)} %get-tuple-element.46), channel_id=1, source_target_pairs={{0,16},{16,32},{32,48},{48,64},{64,80},{80,96},{96,112},{112,128},... | collective-permute-start | bytes 49160 | tf_op jit(solution)/shard_map/ppermute | solution.py:25
  163.6 7.5 %collective-permute-start.5 = (f32[2,2,1024]{2,1,0:T(2,128)S(1)}, f32[2,2,1024]{2,1,0:T(2,128)S(1)}, u32[]{:S(2)}, u32[]{:S(2)}) collective-permute-start(f32[2,2,1024]{2,1,0:T(2,128)S(1)} %get-tuple-element.47), channel_id=1, source_target_pairs={{16,0},{32,16},{48,32},{64,48},{80,64},{96,80},{112,96},{128,112},... | collective-permute-start | bytes 49160 | tf_op jit(solution)/shard_map/ppermute | solution.py:27
  168.9 4.0 %copy-start = (f32[16,2,16,1024]{3,2,1,0:T(8,128)S(1)}, f32[16,2,16,1024]{3,2,1,0:T(8,128)}, u32[]{:S(2)}) copy-start(f32[16,2,16,1024]{3,2,1,0:T(8,128)} %param.9) | copy-start | bytes 6291460
  168.9 3.9 %copy-start.1 = (f32[16,2,16,992]{3,0,2,1:T(8,128)S(1)}, f32[16,2,16,992]{3,0,2,1:T(8,128)}, u32[]{:S(2)}) copy-start(f32[16,2,16,992]{3,0,2,1:T(8,128)} %slice.328) | copy-start | bytes 6094852
  182.8 10.3 %collective-permute-start.6 = (f32[16,2,2,1024]{3,0,2,1:T(8,128)S(1)}, f32[16,2,2,1024]{3,0,2,1:T(8,128)S(1)}, u32[]{:S(2)}, u32[]{:S(2)}) collective-permute-start(f32[16,2,2,1024]{3,0,2,1:T(8,128)S(1)} %get-tuple-element.25), channel_id=1, source_target_pairs={{0,16},{16,32},{32,48},{48,64},{64,80},{80,96},{96,112},{112,128},... | collective-permute-start | bytes 786440 | tf_op jit(solution)/shard_map/ppermute | solution.py:25
  182.8 12.4 %collective-permute-start.7 = (f32[16,2,2,1024]{3,0,2,1:T(8,128)S(1)}, f32[16,2,2,1024]{3,0,2,1:T(8,128)S(1)}, u32[]{:S(2)}, u32[]{:S(2)}) collective-permute-start(f32[16,2,2,1024]{3,0,2,1:T(8,128)S(1)} %get-tuple-element.26), channel_id=1, source_target_pairs={{16,0},{32,16},{48,32},{64,48},{80,64},{96,80},{112,96},{128,112},... | collective-permute-start | bytes 786440 | tf_op jit(solution)/shard_map/ppermute | solution.py:27
Sparse Core Ops, SparseCore 0:
  9.9 152.3 all-reduce.16
where the time goes:
time: 210 us
  waiting for transfers between devices  141 us (67%)
  other arithmetic  22.1 us (11%)
  starting transfers between devices  16.3 us (8%)
  local copies, waits for them, and re-layouts  15.6 us (7%)
  between operations  14.4 us (7%)
    psum x1, waiting for transfers between devices, spread(): return lax.psum(kept, axis)  134 us
    ppermute x4, starting transfers between devices, padded(): lax.ppermute(head, axis, [((i + 1) % count, i) for i in range(count)])  13.6 us
    add x2, other arithmetic, retreat(): interior + zonal_term + column_mix(interior, row_weight, level_weight)  7.35 us
    slice x6, local copies, waits for them, and re-layouts, forward_shift(): return jnp.concatenate([source[..., offset:], padding], axis=-1)  6.04 us
    mul x3, other arithmetic, column_mix(): row_flux = row_weight * (forward_shift(source, 1) - source)  5.84 us
    ppermute x4, waiting for transfers between devices, padded(): lax.ppermute(tail, axis, [(i, (i + 1) % count) for i in range(count)])  5.32 us
  transfers between devices with their start and end apart: 9, of which 3 were waited for; matrix products, arithmetic and copies ran while one was open for 11% of the time, Pallas kernels for 0%

commit v1 on v0

--- a/solution.py
+++ b/solution.py
@@ -33,7 +33,7 @@
 
 def spread(value, axis, source):
     kept = jnp.where(lax.axis_index(axis) == source, value, 0).astype(value.dtype)
-    return lax.psum(kept, axis)
+    return jnp.sum(lax.all_gather(kept, axis), axis=0)
 
 
 def chemistry(carbon, alkalinity, piston, surface_sea):

time: 210 us -> 109 us (0.52)
  waiting for transfers between devices: 141 us -> 45.8 us
  local copies, waits for them, and re-layouts: 15.6 us -> 12.4 us
  other arithmetic: 22.1 us -> 19.8 us
    psum x1 -> x0, waiting for transfers between devices: 134 us -> none  [spread(): return lax.psum(kept, axis)]
    all_gather x0 -> x1, waiting for transfers between devices: none -> 28.3 us  [spread(): return jnp.sum(lax.all_gather(kept, axis), axis=0)]
    ppermute x4, waiting for transfers between devices: 5.32 us -> 14.9 us  [padded(): lax.ppermute(tail, axis, [(i, (i + 1) % count) for i in range(count)])]
    slice x6, local copies, waits for them, and re-layouts: 6.04 us -> 1.57 us  [forward_shift(): return jnp.concatenate([source[..., offset:], padding], axis=-1)]
    mul x3, other arithmetic: 5.84 us -> 3 us  [column_mix(): row_flux = row_weight * (forward_shift(source, 1) - source)]
    unnamed x10 -> x8, local copies, waits for them, and re-layouts: 2.85 us -> 5.1 us
  transfers between devices with their start and end apart: 9 -> 9, of which waited for: 3 -> 6; matrix products, arithmetic and copies ran while one was open for 11% -> 16% of each run, Pallas kernels for 0% -> 0%
where the time goes in v1:
time: 109 us
  waiting for transfers between devices  45.8 us (42%)
  other arithmetic  19.8 us (18%)
  starting transfers between devices  16.5 us (15%)
  between operations  14.4 us (13%)
  local copies, waits for them, and re-layouts  12.4 us (11%)
    all_gather x1, waiting for transfers between devices, spread(): return jnp.sum(lax.all_gather(kept, axis), axis=0)  28.3 us
    ppermute x4, waiting for transfers between devices, padded(): lax.ppermute(tail, axis, [(i, (i + 1) % count) for i in range(count)])  14.9 us
    ppermute x4, starting transfers between devices, padded(): lax.ppermute(head, axis, [((i + 1) % count, i) for i in range(count)])  12.5 us
    add x2, other arithmetic, retreat(): interior + zonal_term + column_mix(interior, row_weight, level_weight)  7.13 us
    unnamed x8, local copies, waits for them, and re-layouts  5.1 us
    ppermute x4, starting transfers between devices, padded(): lax.ppermute(tail, axis, [(i, (i + 1) % count) for i in range(count)])  4.06 us
    mul x3, other arithmetic, column_mix(): row_flux = row_weight * (forward_shift(source, 1) - source)  3 us
    ppermute x4, waiting for transfers between devices, padded(): lax.ppermute(head, axis, [((i + 1) % count, i) for i in range(count)])  2.6 us
  transfers between devices with their start and end apart: 9, of which 6 were waited for; matrix products, arithmetic and copies ran while one was open for 16% of the time, Pallas kernels for 0%

profile of v1, /device:TPU:1, one launch (start us, length us, event | category | flops | bytes accessed | tf_op | source)
XLA Modules:
  0.0 108.9 jit_solution(2242174303969272847)
XLA Ops:
  6.5 0.0 all-gather.2.cloned.1.call-start
  7.2 1.6 %dynamic-slice_select_fusion = f32[1,2,16,1024]{3,2,1,0:T(8,128)} fusion(f32[4,2,16,1024]{3,2,1,0:T(8,128)} %param.10, s32[]{:T(128)S(6)} %select_n.48, pred[]{:T(512)S(6)} %eq.20), kind=kLoop, calls=%fused_computation.60 | loop fusion | flops 32768 | bytes 262149 | tf_op jit(solution)/shard_map/jit(_where)/select_n | solution.py:35
  8.8 0.0 all-gather.2.cloned.1.call-update
  8.8 0.7 convert_element_type.25
  9.5 0.8 convert_element_type.24
  10.4 1.0 concatenate.75
  11.3 2.1 %collective-permute-start = (f32[2,3168]{1,0:T(2,128)S(1)}, f32[2,3168]{1,0:T(2,128)S(1)}, u32[]{:S(2)}, u32[]{:S(2)}) collective-permute-start(f32[2,3168]{1,0:T(2,128)S(1)} %get-tuple-element.39), channel_id=1, source_target_pairs={{0,16},{16,32},{32,48},{48,64},{64,80},{80,96},{96,112},{112,128},... | collective-permute-start | bytes 76040 | tf_op jit(solution)/shard_map/ppermute | solution.py:25
  13.4 5.4 %collective-permute-start.1 = (f32[2,3168]{1,0:T(2,128)S(1)}, f32[2,3168]{1,0:T(2,128)S(1)}, u32[]{:S(2)}, u32[]{:S(2)}) collective-permute-start(f32[2,3168]{1,0:T(2,128)S(1)} %get-tuple-element.40), channel_id=1, source_target_pairs={{16,0},{32,16},{48,32},{64,48},{80,64},{96,80},{112,96},{128,112},... | collective-permute-start | bytes 76040 | tf_op jit(solution)/shard_map/ppermute | solution.py:27
  18.8 2.8 %copy.14 = f32[16,2,16,1024]{3,0,2,1:T(8,128)S(1)} copy(f32[16,2,16,1024]{3,2,1,0:T(8,128)} %param.9) | data formatting | bytes 4194304 | tf_op args[0]
  21.6 0.8 fusion.64
  22.5 1.4 %collective-permute-start.3 = (f32[16,2,2,1024]{3,0,2,1:T(8,128)}, f32[16,2,2,1024]{3,0,2,1:T(8,128)S(1)}, u32[]{:S(2)}, u32[]{:S(2)}) collective-permute-start(f32[16,2,2,1024]{3,0,2,1:T(8,128)} %get-tuple-element.30), channel_id=1, source_target_pairs={{16,0},{32,16},{48,32},{64,48},{80,64},{96,80},{112,96},{128,112},... | collective-permute-start | bytes 786440 | tf_op jit(solution)/shard_map/ppermute | solution.py:27
  23.8 0.1 collective-permute-start.2
  23.9 0.6 slice.328
  24.5 0.6 slice.322
  25.2 0.0 collective-permute-done
  25.2 0.0 collective-permute-done.1
  25.2 0.1 slice.320
  25.3 0.1 slice.325
  25.4 0.0 copy-start
  25.4 0.1 pad_maximum_fusion.9
  25.6 0.1 multiply_bitcast_fusion.1
  25.7 0.1 select_add_fusion
  25.9 6.8 %collective-permute-done.2 = f32[16,2,2,1024]{3,0,2,1:T(8,128)} collective-permute-done((f32[16,2,2,1024]{3,0,2,1:T(8,128)}, f32[16,2,2,1024]{3,0,2,1:T(8,128)}, u32[]{:S(2)}, u32[]{:S(2)}) %collective-permute-start.2) | collective-permute-done | bytes 262176 | tf_op jit(solution)/shard_map/ppermute | solution.py:25
  32.6 1.0 constant_dynamic-update-slice_fusion.2
  33.6 0.0 copy-done
  33.6 2.1 %subtract_multiply_fusion.3 = (f32[16,2,16,1024]{3,0,2,1:T(8,128)S(1)}, f32[16,2,20,1024]{3,0,2,1:T(8,128)S(1)}, f32[16,2,16,1024]{3,0,2,1:T(8,128)S(1)}) fusion(f32[16,2,16,1023]{3,0,2,1:T(8,128)S(1)} %slice.322, f32[16,1024]{1,0:T(8,128)S(1)} %get-tuple-element.47, f32[16,2,16,1024]{3,2,1,0:T(8,128)S(1)} %copy-done, ...), kind=kLoop, calls=%fused_computation.30 | loop fusion | flops 2097152 | bytes 12713984 | tf_op jit(solution)/shard_map/mul | solution.py:76
  35.7 0.2 collective-permute-done.3
  35.9 0.3 slice_subtract_fusion.1
  36.3 4.4 %fusion.8 = f32[16,2,16,1024]{3,0,2,1:T(8,128)S(1)} fusion(f32[16,2,19,1024]{3,0,2,1:T(8,128)S(1)} %slice_subtract_fusion.1, f32[16,2,16,992]{3,0,2,1:T(8,128)S(1)} %bitcast.347, f32[16,2,16,1024]{3,0,2,1:T(8,128)S(1)} %get-tuple-element.29, f32[16,2,16,1024]{3,0,2,1:T(8,128)S(1)} %get-tuple-element.27, f32[16,2,16,1023]{3,0,2,1:T(8,128)S(1)} %bitcast.346, ...), kind=kLoop, calls=%fused_computation.20 | loop fusion | flops 6291456 | bytes 21166080 | tf_op jit(solution)/shard_map/add | solution.py:137
  40.7 0.0 copy-start.1
  40.7 1.3 %copy-done.1 = f32[16,2,16,1024]{3,0,2,1:T(8,128)} copy-done((f32[16,2,16,1024]{3,0,2,1:T(8,128)}, f32[16,2,16,1024]{3,0,2,1:T(8,128)S(1)}, u32[]{:S(2)}) %copy-start.1) | copy-done | bytes 2097176
  42.0 0.6 slice.357
  42.6 0.0 copy-start.2
  42.6 28.3 %all-gather.2.cloned.1.call-done = f32[16,2,16,1024]{3,2,1,0:T(8,128)} async-done(((f32[1,2,16,1024]{3,2,1,0:T(8,128)}), f32[16,2,16,1024]{3,2,1,0:T(8,128)}) %all-gather.2.cloned.1.call-update) | async-done | bytes 2097168 | tf_op jit(solution)/shard_map/all_gather | solution.py:36
  70.9 1.7 %reduce_sum.9 = f32[2,16,1024]{2,1,0:T(8,128)S(1)} reduce(f32[16,2,16,1024]{3,2,1,0:T(8,128)} %all-gather.2.cloned.1.call-done, f32[]{:T(128)} %constant.118.clone.1), dimensions={0}, to_apply=%region_0.1 | reduce | flops 491520 | bytes 2228228 | tf_op jit(solution)/shard_map/reduce_sum | solution.py:36
  72.7 0.1 slice.346
  72.8 0.1 slice.344
  72.9 0.5 collective-permute-start.4
  73.4 3.3 %collective-permute-start.5 = (f32[2,2,1024]{2,1,0:T(2,128)S(1)}, f32[2,2,1024]{2,1,0:T(2,128)S(1)}, u32[]{:S(2)}, u32[]{:S(2)}) collective-permute-start(f32[2,2,1024]{2,1,0:T(2,128)S(1)} %get-tuple-element.46), channel_id=1, source_target_pairs={{16,0},{32,16},{48,32},{64,48},{80,64},{96,80},{112,96},{128,112},... | collective-permute-start | bytes 49160 | tf_op jit(solution)/shard_map/ppermute | solution.py:27
  76.7 0.0 copy-done.2
  76.8 0.1 add_bitcast_fusion.1
  76.9 0.9 collective-permute-done.4
  77.8 0.0 collective-permute-done.5
  77.8 0.1 fusion.14
  77.9 0.1 fusion.20
  78.1 0.1 slice_bitcast_fusion.6
  78.2 0.1 add_bitcast_fusion
  78.2 0.1 maximum_bitcast_fusion
  78.3 0.1 add_bitcast_fusion.3
  78.5 1.0 slice_add_fusion.1
  79.5 0.2 fusion.11
  79.7 0.7 fusion
  80.4 1.3 %collective-permute-start.6 = (f32[16,2,2,1024]{3,0,2,1:T(8,128)S(1)}, f32[16,2,2,1024]{3,0,2,1:T(8,128)S(1)}, u32[]{:S(2)}, u32[]{:S(2)}) collective-permute-start(f32[16,2,2,1024]{3,0,2,1:T(8,128)S(1)} %get-tuple-element.25), channel_id=1, source_target_pairs={{0,16},{16,32},{32,48},{48,64},{64,80},{80,96},{96,112},{112,128},... | collective-permute-start | bytes 786440 | tf_op jit(solution)/shard_map/ppermute | solution.py:25
  81.7 2.4 %collective-permute-start.7 = (f32[16,2,2,1024]{3,0,2,1:T(8,128)S(1)}, f32[16,2,2,1024]{3,0,2,1:T(8,128)S(1)}, u32[]{:S(2)}, u32[]{:S(2)}) collective-permute-start(f32[16,2,2,1024]{3,0,2,1:T(8,128)S(1)} %get-tuple-element.26), channel_id=1, source_target_pairs={{16,0},{32,16},{48,32},{64,48},{80,64},{96,80},{112,96},{128,112},... | collective-permute-start | bytes 786440 | tf_op jit(solution)/shard_map/ppermute | solution.py:27
  84.1 0.9 subtract_multiply_fusion.1
  85.0 0.1 select_add_fusion.1
  85.1 7.2 %collective-permute-done.6 = f32[16,2,2,1024]{3,0,2,1:T(8,128)S(1)} collective-permute-done((f32[16,2,2,1024]{3,0,2,1:T(8,128)S(1)}, f32[16,2,2,1024]{3,0,2,1:T(8,128)S(1)}, u32[]{:S(2)}, u32[]{:S(2)}) %collective-permute-start.6) | collective-permute-done | bytes 262176 | tf_op jit(solution)/shard_map/ppermute | solution.py:25
  92.3 2.4 %collective-permute-done.7 = f32[16,2,2,1024]{3,0,2,1:T(8,128)S(1)} collective-permute-done((f32[16,2,2,1024]{3,0,2,1:T(8,128)S(1)}, f32[16,2,2,1024]{3,0,2,1:T(8,128)S(1)}, u32[]{:S(2)}, u32[]{:S(2)}) %collective-permute-start.7) | collective-permute-done | bytes 262176 | tf_op jit(solution)/shard_map/ppermute | solution.py:27
  94.7 0.6 pad_maximum_fusion.1
  95.3 0.2 slice_subtract_fusion
  95.5 2.7 %fusion.3 = f32[16,2,16,1024]{3,0,2,1:T(8,128)S(1)} fusion(f32[16,2,19,1024]{3,0,2,1:T(8,128)S(1)} %slice_subtract_fusion, f32[16,2,16,992]{3,0,2,1:T(8,128)S(1)} %bitcast.348, f32[16,2,16,1024]{3,0,2,1:T(8,128)S(1)} %get-tuple-element.23, f32[16,2,16,1023]{3,0,2,1:T(8,128)S(1)} %bitcast.345, f32[16,2,16,992]{3,0,2,1:T(8,128)S(1)} %slice.357, ...), kind=kLoop, calls=%fused_computation.11 | loop fusion | flops 7864320 | bytes 19134464 | tf_op jit(solution)/shard_map/add | solution.py:137
  98.3 0.6 slice.374
  98.9 0.6 pad_maximum_fusion.2
  99.6 2.5 %copy.20 = f32[16,2,16,1024]{3,2,1,0:T(8,128)} copy(f32[16,2,16,1024]{3,0,2,1:T(8,128)S(1)} %pad_maximum_fusion.2) | data formatting | bytes 4194304 | tf_op jit(solution)/shard_map/concatenate | solution.py:140
  (21 shorter events, 0.4 us)
Async XLA Ops:
  6.5 64.4 %all-gather.2.cloned.1.call-start = ((), (), s32[]{:S(2)}) async-start(), calls=%async_computation | async-start | bytes 2228224 | tf_op jit(solution)/shard_map/all_gather | solution.py:36
  11.3 13.8 %collective-permute-start = (f32[2,3168]{1,0:T(2,128)S(1)}, f32[2,3168]{1,0:T(2,128)S(1)}, u32[]{:S(2)}, u32[]{:S(2)}) collective-permute-start(f32[2,3168]{1,0:T(2,128)S(1)} %get-tuple-element.39), channel_id=1, source_target_pairs={{0,16},{16,32},{32,48},{48,64},{64,80},{80,96},{96,112},{112,128},... | collective-permute-start | bytes 76040 | tf_op jit(solution)/shard_map/ppermute | solution.py:25
  13.4 11.7 %collective-permute-start.1 = (f32[2,3168]{1,0:T(2,128)S(1)}, f32[2,3168]{1,0:T(2,128)S(1)}, u32[]{:S(2)}, u32[]{:S(2)}) collective-permute-start(f32[2,3168]{1,0:T(2,128)S(1)} %get-tuple-element.40), channel_id=1, source_target_pairs={{16,0},{32,16},{48,32},{64,48},{80,64},{96,80},{112,96},{128,112},... | collective-permute-start | bytes 76040 | tf_op jit(solution)/shard_map/ppermute | solution.py:27
  22.5 13.5 %collective-permute-start.3 = (f32[16,2,2,1024]{3,0,2,1:T(8,128)}, f32[16,2,2,1024]{3,0,2,1:T(8,128)S(1)}, u32[]{:S(2)}, u32[]{:S(2)}) collective-permute-start(f32[16,2,2,1024]{3,0,2,1:T(8,128)} %get-tuple-element.30), channel_id=1, source_target_pairs={{16,0},{32,16},{48,32},{64,48},{80,64},{96,80},{112,96},{128,112},... | collective-permute-start | bytes 786440 | tf_op jit(solution)/shard_map/ppermute | solution.py:27
  23.8 8.8 %collective-permute-start.2 = (f32[16,2,2,1024]{3,0,2,1:T(8,128)}, f32[16,2,2,1024]{3,0,2,1:T(8,128)}, u32[]{:S(2)}, u32[]{:S(2)}) collective-permute-start(f32[16,2,2,1024]{3,0,2,1:T(8,128)} %get-tuple-element.31), channel_id=1, source_target_pairs={{0,16},{16,32},{32,48},{48,64},{64,80},{80,96},{96,112},{112,128},... | collective-permute-start | bytes 786440 | tf_op jit(solution)/shard_map/ppermute | solution.py:25
  25.4 8.2 %copy-start = (f32[16,2,16,1024]{3,2,1,0:T(8,128)S(1)}, f32[16,2,16,1024]{3,2,1,0:T(8,128)}, u32[]{:S(2)}) copy-start(f32[16,2,16,1024]{3,2,1,0:T(8,128)} %param.9) | copy-start | bytes 6291460
  40.7 1.3 %copy-start.1 = (f32[16,2,16,1024]{3,0,2,1:T(8,128)}, f32[16,2,16,1024]{3,0,2,1:T(8,128)S(1)}, u32[]{:S(2)}) copy-start(f32[16,2,16,1024]{3,0,2,1:T(8,128)S(1)} %fusion.8) | copy-start | bytes 6291460
  42.6 34.1 %copy-start.2 = (f32[16,32]{1,0:T(8,128)S(1)}, f32[16,32]{1,0:T(8,128)}, u32[]{:S(2)}) copy-start(f32[16,32]{1,0:T(8,128)} %param.15) | copy-start | bytes 6148
  72.9 5.0 %collective-permute-start.4 = (f32[2,2,1024]{2,1,0:T(2,128)S(1)}, f32[2,2,1024]{2,1,0:T(2,128)S(1)}, u32[]{:S(2)}, u32[]{:S(2)}) collective-permute-start(f32[2,2,1024]{2,1,0:T(2,128)S(1)} %get-tuple-element.45), channel_id=1, source_target_pairs={{0,16},{16,32},{32,48},{48,64},{64,80},{80,96},{96,112},{112,128},... | collective-permute-start | bytes 49160 | tf_op jit(solution)/shard_map/ppermute | solution.py:25
  73.4 4.4 %collective-permute-start.5 = (f32[2,2,1024]{2,1,0:T(2,128)S(1)}, f32[2,2,1024]{2,1,0:T(2,128)S(1)}, u32[]{:S(2)}, u32[]{:S(2)}) collective-permute-start(f32[2,2,1024]{2,1,0:T(2,128)S(1)} %get-tuple-element.46), channel_id=1, source_target_pairs={{16,0},{32,16},{48,32},{64,48},{80,64},{96,80},{112,96},{128,112},... | collective-permute-start | bytes 49160 | tf_op jit(solution)/shard_map/ppermute | solution.py:27
  80.4 11.9 %collective-permute-start.6 = (f32[16,2,2,1024]{3,0,2,1:T(8,128)S(1)}, f32[16,2,2,1024]{3,0,2,1:T(8,128)S(1)}, u32[]{:S(2)}, u32[]{:S(2)}) collective-permute-start(f32[16,2,2,1024]{3,0,2,1:T(8,128)S(1)} %get-tuple-element.25), channel_id=1, source_target_pairs={{0,16},{16,32},{32,48},{48,64},{64,80},{80,96},{96,112},{112,128},... | collective-permute-start | bytes 786440 | tf_op jit(solution)/shard_map/ppermute | solution.py:25
  81.7 13.0 %collective-permute-start.7 = (f32[16,2,2,1024]{3,0,2,1:T(8,128)S(1)}, f32[16,2,2,1024]{3,0,2,1:T(8,128)S(1)}, u32[]{:S(2)}, u32[]{:S(2)}) collective-permute-start(f32[16,2,2,1024]{3,0,2,1:T(8,128)S(1)} %get-tuple-element.26), channel_id=1, source_target_pairs={{16,0},{32,16},{48,32},{64,48},{80,64},{96,80},{112,96},{128,112},... | collective-permute-start | bytes 786440 | tf_op jit(solution)/shard_map/ppermute | solution.py:27
Sparse Core Ops, SparseCore 0:
  10.1 60.7 all-gather.1
